TPU v7x, 256 devices: a whole 4x4x8 slice. The times are simulated.
256 devices in a mesh: row: 16 (over z_hi, y, core), col: 16 (over x, z_lo).
Axes of the slice: x: 4, y: 4, z: 8 (z_hi: 2, z_lo: 4; z = z_hi * 4 + z_lo), core: 2. Of those that a mesh axis runs over, the one named last changes fastest.
Arguments:
- coefficients: float32 [8192, 8192], P('row', 'col'), may hold values from -6 to 6
- alpha_pattern: int32 [16, 10], P('row'), may hold values from 0 to 15, all different within a row
- alpha_count: int32 [16], P('row'), may hold values from 1 to 10
- alpha_blocks: bfloat16 [16, 10, 512, 512], P('row'), may hold values from -0.078125 to 0.078125
- beta_pattern: int32 [16, 10], P('col'), may hold values from 0 to 15, all different within a row
- beta_count: int32 [16], P('col'), may hold values from 1 to 10
- beta_blocks: bfloat16 [16, 10, 512, 512], P('col'), may hold values from -0.078125 to 0.078125
Outputs:
- sigma: float32 [8192, 8192], P('row', 'col')
Inputs may be any that keep to these rules, and one draw needn't show every extreme that they name: `alpha_pattern`: each row lists 10 different blocks, and every block stands in some row. `beta_pattern`: each row lists 10 different blocks, and every block stands in some row.
All inputs are finite; a program needn't handle non-finite values.
Results may differ from a plain program's by a relative error of at most 0.0029.
Values may be sent and summed in bfloat16 or wider, within the bound.
No kernel may reach another device: no remote copies, remote signals or barrier semaphores. Data moves between devices by JAX's collectives and lax.ppermute only.
A program may use at most 128 MiB of HBM per device.

v0:
```python
import jax
import jax.numpy as jnp
from jax import lax
from jax.sharding import PartitionSpec as P


def slot_mask(count, slots):
    return lax.broadcasted_iota(jnp.int32, (count.shape[0], slots), 1) < count[:, None]


def body(
    coefficients, alpha_pattern, alpha_count, alpha_blocks, beta_pattern, beta_count, beta_blocks
):
    coeff_bf = coefficients.astype(jnp.bfloat16)
    tile_rows, tile_cols = coeff_bf.shape
    slots = alpha_blocks.shape[1]
    block = alpha_blocks.shape[2]
    strings = tile_rows * lax.axis_size("row")
    blocks_all = strings // block
    alpha_mask = slot_mask(alpha_count, slots).astype(jnp.bfloat16)
    beta_mask = slot_mask(beta_count, slots).astype(jnp.bfloat16)
    column_slab = lax.all_gather(coeff_bf, "row", axis=0, tiled=True)
    row_slab = lax.all_gather(coeff_bf, "col", axis=1, tiled=True)
    slab_blocks = column_slab.reshape(blocks_all, block, tile_cols)
    slab_cols = row_slab.reshape(tile_rows, blocks_all, block)
    weighted = alpha_blocks * alpha_mask[:, :, None, None]
    picked = slab_blocks[alpha_pattern]
    alpha_term = jnp.einsum("itab,itbc->iac", weighted, picked, preferred_element_type=jnp.float32)
    beta_weighted = beta_blocks * beta_mask[:, :, None, None]
    beta_picked = slab_cols[:, beta_pattern, :]
    beta_term = jnp.einsum(
        "abtk,btck->bac", beta_picked, beta_weighted, preferred_element_type=jnp.float32
    )
    alpha_term = alpha_term.reshape(tile_rows, tile_cols)
    beta_term = jnp.transpose(beta_term, (1, 0, 2)).reshape(tile_rows, tile_cols)
    return alpha_term + beta_term


def solution(mesh):
    placed = (
        P("row", "col"),
        P("row", None),
        P("row"),
        P("row", None, None, None),
        P("col", None),
        P("col"),
        P("col", None, None, None),
    )
    return jax.shard_map(
        body, mesh=mesh, in_specs=placed, out_specs=P("row", "col"), check_vma=False
    )
```

profile of v0, /device:TPU:1, one launch (start us, length us, event | category | flops | bytes accessed | tf_op | source)
XLA Modules:
  0.0 356.1 jit_solution(14214862564943844612)
XLA Ops:
  6.5 0.0 all-gather.5.cloned.1.call-start
  6.5 2.2 copy.10
  8.8 0.0 all-gather.5.cloned.1.call-update
  8.8 0.0 all-gather.3.cloned.1.call-start
  8.8 0.7 all-gather.3.cloned.1.call-update
  10.9 0.7 fusion.22
  11.5 0.7 fusion.23
  12.2 185.9 %all-gather.5.cloned.1.call-done = bf16[512,8192]{0,1:T(8,128)(2,1)} async-done(((bf16[512,512]{0,1:T(8,128)(2,1)}), bf16[512,8192]{0,1:T(8,128)(2,1)}) %all-gather.5.cloned.1.call-update) | async-done | bytes 8388624 | tf_op jit(solution)/shard_map/all_gather | solution.py:23
  198.1 12.3 %copy.12 = bf16[512,16,512]{2,0,1:T(8,128)(2,1)} copy(bf16[512,16,512]{0,2,1:T(8,128)(2,1)} %bitcast.37) | data formatting | bytes 16777216 | tf_op jit(solution)/shard_map/reshape | solution.py:25
  210.4 101.7 %all-gather.3.cloned.1.call-done = bf16[8192,512]{0,1:T(8,128)(2,1)} async-done(((bf16[512,512]{0,1:T(8,128)(2,1)}), bf16[8192,512]{0,1:T(8,128)(2,1)}) %all-gather.3.cloned.1.call-update) | async-done | bytes 8388624 | tf_op jit(solution)/shard_map/all_gather | solution.py:22
  312.1 11.9 %copy.11 = bf16[8192,512]{1,0:T(8,128)(2,1)} copy(bf16[8192,512]{0,1:T(8,128)(2,1)} %all-gather.3.cloned.1.call-done) | data formatting | bytes 16777216 | tf_op jit(solution)/shard_map/all_gather | solution.py:22
  324.0 7.2 %gather_fusion = bf16[10,512,512]{2,1,0:T(8,128)(2,1)} fusion(bf16[16,512,512]{2,1,0:T(8,128)(2,1)} %bitcast.36, s32[1024]{0:T(1024)S(1)} %pad_clamp_fusion.1), kind=kCustom, calls=%fused_computation | custom fusion | bytes 10485800 | tf_op jit(solution)/shard_map/gather | solution.py:27
  331.2 0.0 slice-start
  331.2 7.3 %gather_fusion.1 = bf16[10,512,512]{2,1,0:T(8,128)(2,1)} fusion(bf16[512,16,512]{2,0,1:T(8,128)(2,1)} %copy.12, s32[1024]{0:T(1024)S(1)} %pad_clamp_fusion), kind=kCustom, calls=%fused_computation.1 | custom fusion | bytes 10485800 | tf_op jit(solution)/shard_map/gather | solution.py:30
  338.5 0.0 copy-start
  338.5 0.0 slice-start.1
  338.6 6.6 %fusion.9 = f32[512,512]{1,0:T(8,128)S(1)} fusion(bf16[10,512,512]{2,1,0:T(8,128)(2,1)} %gather_fusion, bf16[1,10,512,512]{3,2,1,0:T(8,128)(2,1)} %param.10, bf16[10]{0:T(256)(128)(2,1)S(1)} %compare_convert_fusion.1), kind=kOutput, calls=%fused_computation.11 | convolution fusion | flops 2686976000 | bytes 11534356 | tf_op jit(solution)/shard_map/itab,itbc->iac/dot_general | solution.py:28
  345.1 0.0 slice-done
  345.1 0.0 copy-done
  345.1 0.2 slice-done.1
  345.3 4.0 %fusion.17 = f32[512,512]{1,0:T(8,128)} fusion(f32[512,512]{1,0:T(8,128)S(1)} %fusion.9, bf16[1,10,512,512]{3,2,1,0:T(8,128)(2,1)S(1)} %bitcast.39, bf16[10]{0:T(256)(128)(2,1)S(1)} %compare_convert_fusion, bf16[10,512,512]{2,1,0:T(8,128)(2,1)S(1)} %copy-done), kind=kOutput, calls=%fused_computation.13 | convolution fusion | flops 2687238144 | bytes 12582932 | tf_op jit(solution)/shard_map/abtk,btck->bac/dot_general | solution.py:31
  (5 shorter events, 0.0 us)
Async XLA Ops:
  6.5 191.5 %all-gather.5.cloned.1.call-start = ((), (), s32[]{:S(2)}) async-start(), calls=%async_computation.1 | async-start | bytes 8912896 | tf_op jit(solution)/shard_map/all_gather | solution.py:23
  8.8 303.3 %all-gather.3.cloned.1.call-start = ((), (), s32[]{:S(2)}) async-start(), calls=%async_computation | async-start | bytes 8912896 | tf_op jit(solution)/shard_map/all_gather | solution.py:22
  331.2 13.9 %slice-start = ((s8[5242880]{0:T(1024)(128)(4,1)}), s8[1048576]{0:T(1024)(128)(4,1)S(1)}, s32[]{:S(2)}) async-start(s8[5242880]{0:T(1024)(128)(4,1)} %bitcast.38), calls=%async_computation.2 | async-start | bytes 2097152
  338.5 6.6 %copy-start = (bf16[10,512,512]{2,1,0:T(8,128)(2,1)S(1)}, bf16[10,512,512]{2,1,0:T(8,128)(2,1)}, u32[]{:S(2)}) copy-start(bf16[10,512,512]{2,1,0:T(8,128)(2,1)} %gather_fusion.1) | copy-start | bytes 15728644
  338.5 6.8 %slice-start.1 = ((s8[5242880]{0:T(1024)(128)(4,1)}), s8[4194304]{0:T(1024)(128)(4,1)S(1)}, s32[]{:S(2)}) async-start(s8[5242880]{0:T(1024)(128)(4,1)} %bitcast.38), calls=%async_computation.3 | async-start | bytes 8388608
Sparse Core Ops, SparseCore 0:
  9.1 188.8 all-gather.4
  200.6 111.4 all-gather.2
where the time goes:
time: 357 us; the launch traced here: 356 us
  waiting for transfers between devices  288 us (81%)
  local copies, waits for them, and re-layouts  41.2 us (12%)
  between operations  14.7 us (4%)
  matrix products  10.5 us (3%)
    all_gather x1, waiting for transfers between devices, body(): row_slab = lax.all_gather(coeff_bf, 'col', axis=1, tiled=True)  186 us
    all_gather x1, waiting for transfers between devices, body(): column_slab = lax.all_gather(coeff_bf, 'row', axis=0, tiled=True)  102 us
    reshape x1, local copies, waits for them, and re-layouts, body(): slab_cols = row_slab.reshape(tile_rows, blocks_all, block)  12.3 us
    all_gather x1, local copies, waits for them, and re-layouts, body(): column_slab = lax.all_gather(coeff_bf, 'row', axis=0, tiled=True)  11.9 us
    gather x1, local copies, waits for them, and re-layouts, body(): beta_picked = slab_cols[:, beta_pattern, :]  7.34 us
    gather x1, local copies, waits for them, and re-layouts, body(): picked = slab_blocks[alpha_pattern]  7.22 us
  transfers between devices with their start and end apart: 2, of which 2 were waited for; matrix products, arithmetic and copies ran while one was open for 4% of the time, Pallas kernels for 0%

commit v1 on v0

v1 whole, which is shorter than its diff:
```python
import jax
import jax.numpy as jnp
from jax import lax
from jax.sharding import Mesh, PartitionSpec as P

ROW = ("zh", "y", "core")
COL = ("x", "zl")
ROWMODE = "pp"
COLMODE = "pp"


def slot_mask(count, slots):
    return lax.broadcasted_iota(jnp.int32, (count.shape[0], slots), 1) < count[:, None]


def shifts(x, axis):
    n = lax.axis_size(axis)
    out = [x]
    for s in range(1, n):
        out.append(lax.ppermute(x, axis, [(i, (i + s) % n) for i in range(n)]))
    return jnp.stack(out, axis=0)


def row_tiles(t):
    if ROWMODE == "sc":
        slab = lax.all_gather(t, ROW, axis=0, tiled=False)
        return slab.reshape((-1,) + t.shape), lambda p: p
    zh = lax.axis_index("zh"); y = lax.axis_index("y"); core = lax.axis_index("core")
    a1 = shifts(t, "zh")
    a2 = shifts(a1, "y")
    a3 = shifts(a2, "core")
    slab = a3.reshape((-1,) + t.shape)
    def pos(p):
        k1 = (p // 8) ^ zh
        k2 = (y - (p // 2) % 4) % 4
        k3 = (p % 2) ^ core
        return k3 * 8 + k2 * 2 + k1
    return slab, pos


def col_tiles(t):
    if COLMODE == "sc":
        slab = lax.all_gather(t, COL, axis=0, tiled=False)
        return slab.reshape((-1,) + t.shape), lambda q: q
    x = lax.axis_index("x"); zl = lax.axis_index("zl")
    b1 = shifts(t, "zl")
    b2 = shifts(b1, "x")
    slab = b2.reshape((-1,) + t.shape)
    def pos(q):
        k1 = (zl - q % 4) % 4
        k2 = (x - q // 4) % 4
        return k2 * 4 + k1
    return slab, pos


def body(coefficients, alpha_pattern, alpha_count, alpha_blocks, beta_pattern, beta_count, beta_blocks):
    coeff_bf = coefficients.astype(jnp.bfloat16)
    slots = alpha_blocks.shape[1]
    alpha_mask = slot_mask(alpha_count, slots).astype(jnp.bfloat16)
    beta_mask = slot_mask(beta_count, slots).astype(jnp.bfloat16)
    rslab, rpos = row_tiles(coeff_bf)
    cslab, cpos = col_tiles(coeff_bf)
    a_picked = rslab[rpos(alpha_pattern[0])]
    b_picked = cslab[cpos(beta_pattern[0])]
    a_w = alpha_blocks[0] * alpha_mask[0][:, None, None]
    b_w = beta_blocks[0] * beta_mask[0][:, None, None]
    alpha_term = jnp.einsum("tab,tbn->an", a_w, a_picked, preferred_element_type=jnp.float32)
    beta_term = jnp.einsum("tak,tck->ac", b_picked, b_w, preferred_element_type=jnp.float32)
    return alpha_term + beta_term


def solution(mesh):
    fine = Mesh(mesh.devices.reshape(2, 4, 2, 4, 4), ROW + COL)
    placed = (P(ROW, COL), P(ROW, None), P(ROW), P(ROW, None, None, None), P(COL, None), P(COL), P(COL, None, None, None))
    return jax.shard_map(body, mesh=fine, in_specs=placed, out_specs=P(ROW, COL), check_vma=False)
```

time: 357 us -> 227 us (0.64)
  waiting for transfers between devices: 288 us -> 131 us
  starting transfers between devices: 0.04 us -> 43.3 us
  local copies, waits for them, and re-layouts: 41.2 us -> 14.4 us
  other arithmetic: 1.34 us -> 21 us
  between operations: 14.7 us -> 1.41 us
  matrix products: 10.5 us -> 14.7 us
    all_gather x2 -> x0, waiting for transfers between devices: 288 us -> none  [the longest x1 186 us: body(): row_slab = lax.all_gather(coeff_bf, 'col', axis=1, tiled=True)]
    ppermute x0 -> x11, waiting for transfers between devices: none -> 131 us  [shifts(): out.append(lax.ppermute(x, axis, [(i, (i + s) % n) for i in range(n)]))]
    ppermute x0 -> x11, starting transfers between devices: none -> 43.3 us  [shifts(): out.append(lax.ppermute(x, axis, [(i, (i + s) % n) for i in range(n)]))]
    another operation x0 -> x6, other arithmetic: none -> 19.6 us  [shifts(): return jnp.stack(out, axis=0)]
    reshape x1 -> x0, local copies, waits for them, and re-layouts: 12.3 us -> none  [body(): slab_cols = row_slab.reshape(tile_rows, blocks_all, block)]
    all_gather x1 -> x0, local copies, waits for them, and re-layouts: 11.9 us -> none  [body(): column_slab = lax.all_gather(coeff_bf, 'row', axis=0, tiled=True)]
    dot_general x2, matrix products: 10.5 us -> 14.7 us  [the longest x1 7.93 us: body(): jnp.einsum('tab,tbn->an', a_w, a_picked, preferred_element_type=jnp.float32)]
  transfers between devices with their start and end apart: 2 -> 11, of which waited for: 2 -> 6; matrix products, arithmetic and copies ran while one was open for 4% -> 12% of each run, Pallas kernels for 0% -> 0%
where the time goes in v1:
time: 227 us; the launch traced here: 226 us
  waiting for transfers between devices  131 us (58%)
  starting transfers between devices  43.3 us (19%)
  other arithmetic  21 us (9%)
  matrix products  14.7 us (6%)
  local copies, waits for them, and re-layouts  14.4 us (6%)
    ppermute x11, waiting for transfers between devices, shifts(): out.append(lax.ppermute(x, axis, [(i, (i + s) % n) for i in range(n)]))  131 us
    ppermute x11, starting transfers between devices, shifts(): out.append(lax.ppermute(x, axis, [(i, (i + s) % n) for i in range(n)]))  43.3 us
    another operation x6, other arithmetic, shifts(): return jnp.stack(out, axis=0)  19.6 us
    dot_general x1, matrix products, body(): jnp.einsum('tab,tbn->an', a_w, a_picked, preferred_element_type=jnp.float32)  7.93 us
    gather x1, local copies, waits for them, and re-layouts, body(): b_picked = cslab[cpos(beta_pattern[0])]  7.21 us
    gather x1, local copies, waits for them, and re-layouts, body(): a_picked = rslab[rpos(alpha_pattern[0])]  7.21 us
    dot_general x1, matrix products, body(): jnp.einsum('tak,tck->ac', b_picked, b_w, preferred_element_type=jnp.float32)  6.81 us
  transfers between devices with their start and end apart: 11, of which 6 were waited for; matrix products, arithmetic and copies ran while one was open for 12% of the time, Pallas kernels for 0%

profile of v1, /device:TPU:1, one launch (start us, length us, event | category | flops | bytes accessed | tf_op | source)
XLA Modules:
  0.0 226.0 jit_solution(15311662553572953253)
XLA Ops:
  0.0 1.3 convert_element_type.22
  1.3 7.8 %collective-permute-start = (bf16[512,512]{1,0:T(8,128)(2,1)S(1)}, bf16[512,512]{1,0:T(8,128)(2,1)S(1)}, u32[]{:S(2)}, u32[]{:S(2)}) collective-permute-start(bf16[512,512]{1,0:T(8,128)(2,1)S(1)} %convert_element_type.22), channel_id=1, source_target_pairs={{0,128},{128,0},{1,129},{129,1},{2,130},{130,2},{3,131},{131,3},{4... | collective-permute-start | bytes 1572872 | tf_op jit(solution)/shard_map/ppermute | solution.py:20
  9.1 1.3 convert_bitcast_fusion
  10.4 12.0 %collective-permute-done = bf16[512,512]{1,0:T(8,128)(2,1)S(1)} collective-permute-done((bf16[512,512]{1,0:T(8,128)(2,1)S(1)}, bf16[512,512]{1,0:T(8,128)(2,1)S(1)}, u32[]{:S(2)}, u32[]{:S(2)}) %collective-permute-start) | collective-permute-done | bytes 524320 | tf_op jit(solution)/shard_map/ppermute | solution.py:20
  22.4 0.1 fusion.22
  22.5 3.3 %collective-permute-start.3 = (bf16[2,512,512]{2,1,0:T(8,128)(2,1)S(1)}, bf16[2,512,512]{2,1,0:T(8,128)(2,1)S(1)}, u32[]{:S(2)}, u32[]{:S(2)}) collective-permute-start(bf16[2,512,512]{2,1,0:T(8,128)(2,1)S(1)} %get-tuple-element.10), channel_id=1, source_target_pairs={{0,96},{32,0},{64,32},{96,64},{1,97},{33,1},{65,33},{97,65},{2,98}... | collective-permute-start | bytes 3145736 | tf_op jit(solution)/shard_map/ppermute | solution.py:20
  25.8 0.3 collective-permute-start.2
  26.1 0.7 collective-permute-start.1
  26.8 6.6 %collective-permute-start.7 = (bf16[512,512]{1,0:T(8,128)(2,1)S(1)}, bf16[512,512]{1,0:T(8,128)(2,1)S(1)}, u32[]{:S(2)}, u32[]{:S(2)}) collective-permute-start(bf16[512,512]{1,0:T(8,128)(2,1)S(1)} %convert_element_type.22), channel_id=1, source_target_pairs={{0,3},{1,0},{2,1},{3,2},{4,7},{5,4},{6,5},{7,6},{8,11},{9,8},{10,9... | collective-permute-start | bytes 1572872 | tf_op jit(solution)/shard_map/ppermute | solution.py:20
  33.4 4.5 %collective-permute-start.6 = (bf16[512,512]{1,0:T(8,128)(2,1)S(1)}, bf16[512,512]{1,0:T(8,128)(2,1)S(1)}, u32[]{:S(2)}, u32[]{:S(2)}) collective-permute-start(bf16[512,512]{1,0:T(8,128)(2,1)S(1)} %convert_element_type.22), channel_id=1, source_target_pairs={{0,2},{1,3},{2,0},{3,1},{4,6},{5,7},{6,4},{7,5},{8,10},{9,11},{10,... | collective-permute-start | bytes 1572872 | tf_op jit(solution)/shard_map/ppermute | solution.py:20
  37.9 10.4 %collective-permute-done.3 = bf16[2,512,512]{2,1,0:T(8,128)(2,1)S(1)} collective-permute-done((bf16[2,512,512]{2,1,0:T(8,128)(2,1)S(1)}, bf16[2,512,512]{2,1,0:T(8,128)(2,1)S(1)}, u32[]{:S(2)}, u32[]{:S(2)}) %collective-permute-start.3) | collective-permute-done | bytes 1048608 | tf_op jit(solution)/shard_map/ppermute | solution.py:20
  48.3 9.6 %collective-permute-start.5 = (bf16[512,512]{1,0:T(8,128)(2,1)S(1)}, bf16[512,512]{1,0:T(8,128)(2,1)S(1)}, u32[]{:S(2)}, u32[]{:S(2)}) collective-permute-start(bf16[512,512]{1,0:T(8,128)(2,1)S(1)} %convert_element_type.22), channel_id=1, source_target_pairs={{0,1},{1,2},{2,3},{3,0},{4,5},{5,6},{6,7},{7,4},{8,9},{9,10},{10,1... | collective-permute-start | bytes 1572872 | tf_op jit(solution)/shard_map/ppermute | solution.py:20
  57.8 0.0 collective-permute-done.2
  57.8 17.0 %collective-permute-done.1 = bf16[2,512,512]{2,1,0:T(8,128)(2,1)S(1)} collective-permute-done((bf16[2,512,512]{2,1,0:T(8,128)(2,1)S(1)}, bf16[2,512,512]{2,1,0:T(8,128)(2,1)S(1)}, u32[]{:S(2)}, u32[]{:S(2)}) %collective-permute-start.1) | collective-permute-done | bytes 1048608 | tf_op jit(solution)/shard_map/ppermute | solution.py:20
  74.8 3.6 %fusion.24 = (bf16[1,4,2,512,512]{4,3,2,1,0:T(8,128)(2,1)}, bf16[4,2,512,512]{3,2,1,0:T(8,128)(2,1)}) fusion(bf16[1,2,512,512]{3,2,1,0:T(8,128)(2,1)S(1)} %bitcast.84, bf16[1,2,512,512]{3,2,1,0:T(8,128)(2,1)S(1)} %bitcast.85, bf16[1,2,512,512]{3,2,1,0:T(8,128)(2,1)S(1)} %bitcast.86, bf16[1,2,512,512]{3,2,1,0:T(8,128)(2,1)S(1)} %get-tuple-element.9), kind=kLoop, calls=%fused_computation.67 | loop fusion | flops 6291456 | bytes 12582912 | tf_op jit(solution)/shard_map/stack | solution.py:21
  78.5 0.0 copy-start.2
  78.5 0.0 copy-start.1
  78.5 7.0 %collective-permute-start.4 = (bf16[4,2,512,512]{3,2,1,0:T(8,128)(2,1)}, bf16[4,2,512,512]{3,2,1,0:T(8,128)(2,1)}, u32[]{:S(2)}, u32[]{:S(2)}) collective-permute-start(bf16[4,2,512,512]{3,2,1,0:T(8,128)(2,1)} %get-tuple-element.6), channel_id=1, source_target_pairs={{0,16},{16,0},{1,17},{17,1},{2,18},{18,2},{3,19},{19,3},{4,20},{20... | collective-permute-start | bytes 12582920 | tf_op jit(solution)/shard_map/ppermute | solution.py:20
  85.4 0.0 collective-permute-done.7
  85.4 0.0 collective-permute-done.6
  85.4 0.0 collective-permute-done.5
  85.5 1.7 fusion.23
  87.1 2.5 %collective-permute-start.10 = (bf16[4,512,512]{2,1,0:T(8,128)(2,1)}, bf16[4,512,512]{2,1,0:T(8,128)(2,1)}, u32[]{:S(2)}, u32[]{:S(2)}) collective-permute-start(bf16[4,512,512]{2,1,0:T(8,128)(2,1)} %get-tuple-element.8), channel_id=1, source_target_pairs={{0,12},{4,0},{8,4},{12,8},{1,13},{5,1},{9,5},{13,9},{2,14},{6,2},{... | collective-permute-start | bytes 6291464 | tf_op jit(solution)/shard_map/ppermute | solution.py:20
  89.6 0.5 collective-permute-start.9
  90.1 0.6 collective-permute-start.8
  92.1 0.0 copy-done.2
  92.1 0.0 copy-done.1
  92.2 40.5 %collective-permute-done.10 = bf16[4,512,512]{2,1,0:T(8,128)(2,1)} collective-permute-done((bf16[4,512,512]{2,1,0:T(8,128)(2,1)}, bf16[4,512,512]{2,1,0:T(8,128)(2,1)}, u32[]{:S(2)}, u32[]{:S(2)}) %collective-permute-start.10) | collective-permute-done | bytes 2097184 | tf_op jit(solution)/shard_map/ppermute | solution.py:20
  132.7 2.7 %collective-permute-done.9 = bf16[4,512,512]{2,1,0:T(8,128)(2,1)} collective-permute-done((bf16[4,512,512]{2,1,0:T(8,128)(2,1)}, bf16[4,512,512]{2,1,0:T(8,128)(2,1)}, u32[]{:S(2)}, u32[]{:S(2)}) %collective-permute-start.9) | collective-permute-done | bytes 2097184 | tf_op jit(solution)/shard_map/ppermute | solution.py:20
  135.4 48.5 %collective-permute-done.8 = bf16[4,512,512]{2,1,0:T(8,128)(2,1)} collective-permute-done((bf16[4,512,512]{2,1,0:T(8,128)(2,1)}, bf16[4,512,512]{2,1,0:T(8,128)(2,1)}, u32[]{:S(2)}, u32[]{:S(2)}) %collective-permute-start.8) | collective-permute-done | bytes 2097184 | tf_op jit(solution)/shard_map/ppermute | solution.py:20
  183.9 6.7 %pad_maximum_fusion.1 = bf16[4,4,512,512]{3,2,1,0:T(8,128)(2,1)} fusion(bf16[1,4,512,512]{3,2,1,0:T(8,128)(2,1)} %bitcast.20, bf16[1,4,512,512]{3,2,1,0:T(8,128)(2,1)} %bitcast.19, bf16[1,4,512,512]{3,2,1,0:T(8,128)(2,1)} %bitcast.18, bf16[1,4,512,512]{3,2,1,0:T(8,128)(2,1)S(1)} %get-tuple-element.7), kind=kLoop, calls=%fused_computation.3 | loop fusion | flops 12582912 | bytes 16777216 | tf_op jit(solution)/shard_map/stack | solution.py:21
  190.6 7.2 %gather_fusion.1 = bf16[10,512,512]{2,1,0:T(8,128)(2,1)} fusion(bf16[16,512,512]{2,1,0:T(8,128)(2,1)} %bitcast.82, s32[1024]{0:T(1024)S(1)} %pad_clamp_fusion), kind=kCustom, calls=%fused_computation.1 | custom fusion | bytes 10485800 | tf_op jit(solution)/shard_map/gather | solution.py:64
  197.8 0.0 copy-start
  197.8 6.8 %fusion.5 = f32[512,512]{1,0:T(8,128)S(1)} fusion(bf16[10,512,512]{2,1,0:T(8,128)(2,1)} %gather_fusion.1, bf16[1,10,512,512]{3,2,1,0:T(8,128)(2,1)} %param.13, bf16[10]{0:T(256)(128)(2,1)S(1)} %compare_convert_fusion), kind=kOutput, calls=%fused_computation.13 | convolution fusion | flops 2686976000 | bytes 11534356 | tf_op jit(solution)/shard_map/tak,tck->ac/dot_general | solution.py:68
  204.6 0.0 collective-permute-done.4
  204.6 0.0 copy-done
  204.6 6.2 %pad_maximum_fusion = bf16[2,4,2,512,512]{4,3,2,1,0:T(8,128)(2,1)} fusion(bf16[1,4,2,512,512]{4,3,2,1,0:T(8,128)(2,1)} %bitcast.9, bf16[1,4,2,512,512]{4,3,2,1,0:T(8,128)(2,1)S(1)} %copy-done), kind=kLoop, calls=%fused_computation.2 | loop fusion | flops 4194304 | bytes 16777216 | tf_op jit(solution)/shard_map/stack | solution.py:21
  210.9 7.2 %gather_fusion = bf16[10,512,512]{2,1,0:T(8,128)(2,1)} fusion(bf16[16,512,512]{2,1,0:T(8,128)(2,1)} %bitcast.83, s32[1024]{0:T(1024)S(1)} %pad_clamp_fusion.1), kind=kCustom, calls=%fused_computation | custom fusion | bytes 10485800 | tf_op jit(solution)/shard_map/gather | solution.py:63
  218.1 7.9 %fusion.6 = f32[512,512]{1,0:T(8,128)} fusion(f32[512,512]{1,0:T(8,128)S(1)} %fusion.5, bf16[10,512,512]{2,1,0:T(8,128)(2,1)} %gather_fusion, bf16[1,10,512,512]{3,2,1,0:T(8,128)(2,1)} %param.10, bf16[10]{0:T(256)(128)(2,1)S(1)} %compare_convert_fusion.1), kind=kOutput, calls=%fused_computation.14 | convolution fusion | flops 2687238144 | bytes 12582932 | tf_op jit(solution)/shard_map/tab,tbn->an/dot_general | solution.py:67
  (6 shorter events, 0.1 us)
Async XLA Ops:
  1.3 21.1 %collective-permute-start = (bf16[512,512]{1,0:T(8,128)(2,1)S(1)}, bf16[512,512]{1,0:T(8,128)(2,1)S(1)}, u32[]{:S(2)}, u32[]{:S(2)}) collective-permute-start(bf16[512,512]{1,0:T(8,128)(2,1)S(1)} %convert_element_type.22), channel_id=1, source_target_pairs={{0,128},{128,0},{1,129},{129,1},{2,130},{130,2},{3,131},{131,3},{4... | collective-permute-start | bytes 1572872 | tf_op jit(solution)/shard_map/ppermute | solution.py:20
  22.5 25.7 %collective-permute-start.3 = (bf16[2,512,512]{2,1,0:T(8,128)(2,1)S(1)}, bf16[2,512,512]{2,1,0:T(8,128)(2,1)S(1)}, u32[]{:S(2)}, u32[]{:S(2)}) collective-permute-start(bf16[2,512,512]{2,1,0:T(8,128)(2,1)S(1)} %get-tuple-element.10), channel_id=1, source_target_pairs={{0,96},{32,0},{64,32},{96,64},{1,97},{33,1},{65,33},{97,65},{2,98}... | collective-permute-start | bytes 3145736 | tf_op jit(solution)/shard_map/ppermute | solution.py:20
  25.8 32.1 %collective-permute-start.2 = (bf16[2,512,512]{2,1,0:T(8,128)(2,1)S(1)}, bf16[2,512,512]{2,1,0:T(8,128)(2,1)S(1)}, u32[]{:S(2)}, u32[]{:S(2)}) collective-permute-start(bf16[2,512,512]{2,1,0:T(8,128)(2,1)S(1)} %get-tuple-element.10), channel_id=1, source_target_pairs={{0,64},{32,96},{64,0},{96,32},{1,65},{33,97},{65,1},{97,33},{2,66}... | collective-permute-start | bytes 3145736 | tf_op jit(solution)/shard_map/ppermute | solution.py:20
  26.1 48.7 %collective-permute-start.1 = (bf16[2,512,512]{2,1,0:T(8,128)(2,1)S(1)}, bf16[2,512,512]{2,1,0:T(8,128)(2,1)S(1)}, u32[]{:S(2)}, u32[]{:S(2)}) collective-permute-start(bf16[2,512,512]{2,1,0:T(8,128)(2,1)S(1)} %get-tuple-element.10), channel_id=1, source_target_pairs={{0,32},{32,64},{64,96},{96,0},{1,33},{33,65},{65,97},{97,1},{2,34}... | collective-permute-start | bytes 3145736 | tf_op jit(solution)/shard_map/ppermute | solution.py:20
  26.8 58.6 %collective-permute-start.7 = (bf16[512,512]{1,0:T(8,128)(2,1)S(1)}, bf16[512,512]{1,0:T(8,128)(2,1)S(1)}, u32[]{:S(2)}, u32[]{:S(2)}) collective-permute-start(bf16[512,512]{1,0:T(8,128)(2,1)S(1)} %convert_element_type.22), channel_id=1, source_target_pairs={{0,3},{1,0},{2,1},{3,2},{4,7},{5,4},{6,5},{7,6},{8,11},{9,8},{10,9... | collective-permute-start | bytes 1572872 | tf_op jit(solution)/shard_map/ppermute | solution.py:20
  33.4 52.0 %collective-permute-start.6 = (bf16[512,512]{1,0:T(8,128)(2,1)S(1)}, bf16[512,512]{1,0:T(8,128)(2,1)S(1)}, u32[]{:S(2)}, u32[]{:S(2)}) collective-permute-start(bf16[512,512]{1,0:T(8,128)(2,1)S(1)} %convert_element_type.22), channel_id=1, source_target_pairs={{0,2},{1,3},{2,0},{3,1},{4,6},{5,7},{6,4},{7,5},{8,10},{9,11},{10,... | collective-permute-start | bytes 1572872 | tf_op jit(solution)/shard_map/ppermute | solution.py:20
  48.3 37.2 %collective-permute-start.5 = (bf16[512,512]{1,0:T(8,128)(2,1)S(1)}, bf16[512,512]{1,0:T(8,128)(2,1)S(1)}, u32[]{:S(2)}, u32[]{:S(2)}) collective-permute-start(bf16[512,512]{1,0:T(8,128)(2,1)S(1)} %convert_element_type.22), channel_id=1, source_target_pairs={{0,1},{1,2},{2,3},{3,0},{4,5},{5,6},{6,7},{7,4},{8,9},{9,10},{10,1... | collective-permute-start | bytes 1572872 | tf_op jit(solution)/shard_map/ppermute | solution.py:20
  78.5 13.6 %copy-start.2 = (s32[1,10]{1,0:T(1,128)S(1)}, s32[1,10]{1,0:T(1,128)}, u32[]{:S(2)}) copy-start(s32[1,10]{1,0:T(1,128)} %param.11) | copy-start | bytes 124
  78.5 13.6 %copy-start.1 = (s32[1,10]{1,0:T(1,128)S(1)}, s32[1,10]{1,0:T(1,128)}, u32[]{:S(2)}) copy-start(s32[1,10]{1,0:T(1,128)} %param.8) | copy-start | bytes 124
  78.5 126.1 %collective-permute-start.4 = (bf16[4,2,512,512]{3,2,1,0:T(8,128)(2,1)}, bf16[4,2,512,512]{3,2,1,0:T(8,128)(2,1)}, u32[]{:S(2)}, u32[]{:S(2)}) collective-permute-start(bf16[4,2,512,512]{3,2,1,0:T(8,128)(2,1)} %get-tuple-element.6), channel_id=1, source_target_pairs={{0,16},{16,0},{1,17},{17,1},{2,18},{18,2},{3,19},{19,3},{4,20},{20... | collective-permute-start | bytes 12582920 | tf_op jit(solution)/shard_map/ppermute | solution.py:20
  87.1 45.5 %collective-permute-start.10 = (bf16[4,512,512]{2,1,0:T(8,128)(2,1)}, bf16[4,512,512]{2,1,0:T(8,128)(2,1)}, u32[]{:S(2)}, u32[]{:S(2)}) collective-permute-start(bf16[4,512,512]{2,1,0:T(8,128)(2,1)} %get-tuple-element.8), channel_id=1, source_target_pairs={{0,12},{4,0},{8,4},{12,8},{1,13},{5,1},{9,5},{13,9},{2,14},{6,2},{... | collective-permute-start | bytes 6291464 | tf_op jit(solution)/shard_map/ppermute | solution.py:20
  89.6 45.8 %collective-permute-start.9 = (bf16[4,512,512]{2,1,0:T(8,128)(2,1)}, bf16[4,512,512]{2,1,0:T(8,128)(2,1)}, u32[]{:S(2)}, u32[]{:S(2)}) collective-permute-start(bf16[4,512,512]{2,1,0:T(8,128)(2,1)} %get-tuple-element.8), channel_id=1, source_target_pairs={{0,8},{4,12},{8,0},{12,4},{1,9},{5,13},{9,1},{13,5},{2,10},{6,14},... | collective-permute-start | bytes 6291464 | tf_op jit(solution)/shard_map/ppermute | solution.py:20
  90.1 93.8 %collective-permute-start.8 = (bf16[4,512,512]{2,1,0:T(8,128)(2,1)}, bf16[4,512,512]{2,1,0:T(8,128)(2,1)}, u32[]{:S(2)}, u32[]{:S(2)}) collective-permute-start(bf16[4,512,512]{2,1,0:T(8,128)(2,1)} %get-tuple-element.8), channel_id=1, source_target_pairs={{0,4},{4,8},{8,12},{12,0},{1,5},{5,9},{9,13},{13,1},{2,6},{6,10},{... | collective-permute-start | bytes 6291464 | tf_op jit(solution)/shard_map/ppermute | solution.py:20
  197.8 6.8 %copy-start = (bf16[1,4,2,512,512]{4,3,2,1,0:T(8,128)(2,1)S(1)}, bf16[1,4,2,512,512]{4,3,2,1,0:T(8,128)(2,1)}, u32[]{:S(2)}) copy-start(bf16[1,4,2,512,512]{4,3,2,1,0:T(8,128)(2,1)} %get-tuple-element.5) | copy-start | bytes 12582916
